TPU v7x, 128 devices: a whole 4x4x4 slice. The times are simulated.
128 devices in a mesh: req: 8 (over y, core), exp: 16 (over z, x).
Axes of the slice: x: 4, y: 4, z: 4, core: 2. Of those that a mesh axis runs over, the one named last changes fastest.
Arguments:
- hidden: bfloat16 [16384, 2560], P(('req', 'exp')), may hold values from -1.5 to 1.5
- queries: bfloat16 [16384, 1280], P(('req', 'exp')), may hold values from -100 to 100
- suffix_kv: bfloat16 [16384, 512], P(('req', 'exp')), may hold values from -24 to 24
- lengths: int32 [8, 4], P('req'), may hold values from 1 to 1024, 2048 in all within a row
- page_table: int32 [8, 4, 32], P('req'), may hold values from 0 to 55
- page_pool: bfloat16 [56, 128, 512], P('req'), may hold values from -24 to 24
- w_out: bfloat16 [1280, 2560], replicated, may hold values from -0.15625 to 0.15625
- w_router: bfloat16 [2560, 64], replicated, may hold values from -5 to 5
- routes: int32 [16384, 6], P(('req', 'exp')), may hold values from 0 to 63, all different within a row; in each aligned block of 128 rows (0 to 127, 128 to 255, ...) at most 15 rows name the same one
- w_gate: bfloat16 [128, 2560, 768], P(('req', 'exp')), may hold values from -0.125 to 0.125
- w_up: bfloat16 [128, 2560, 768], P(('req', 'exp')), may hold values from -0.125 to 0.125
- w_down: bfloat16 [128, 768, 2560], P(('req', 'exp')), may hold values from -0.4375 to 0.4375
Outputs:
- layer_out: bfloat16 [16384, 2560], P(('req', 'exp'))
Inputs may be any that keep to these rules, and one draw needn't show every extreme that they name: `lengths`: each row sums to 2048; its largest entry is exactly 1024. `page_table`: a page may appear in several prefixes and more than once in one. `routes`: the 6 experts of a token are distinct; among the rows of one device no expert is named more than 15 times, a bound that some block reaches.
All inputs are finite; a program needn't handle non-finite values.
Results may differ from a plain program's by a relative error of at most 0.022.
Values may be sent and summed in bfloat16 or wider, within the bound.
No kernel may reach another device: no remote copies, remote signals or barrier semaphores. Data moves between devices by JAX's collectives and lax.ppermute only.
A program may use at most 192 MiB of HBM per device.

v0:
```python
import math
import jax
import jax.numpy as jnp
from jax import lax
from jax.sharding import PartitionSpec as P

D = 2560
QUERY_HEADS = 10
KEY_VALUE_HEADS = 2
HEAD_SIZE = 128
TOP = 6
PAGE_TOKENS = 128
NEGATIVE_MASK = -1e30
EPS = 1e-06


def fold_scores(carry, query_matrix, key_rows, value_rows, weights):
    scores = jnp.einsum(
        "tgrd,kgd->tgrk", query_matrix, key_rows, preferred_element_type=jnp.float32
    ) * (1.0 / math.sqrt(HEAD_SIZE))
    running_maximum, grand_total, summed_output = carry
    live = weights[:, None, None, :] > 0
    fresh = jnp.maximum(running_maximum, jnp.max(jnp.where(live, scores, NEGATIVE_MASK), axis=-1))
    expo = jnp.where(live, jnp.exp(scores - fresh[..., None]), 0.0) * weights[:, None, None, :]
    decay = jnp.exp(running_maximum - fresh)
    grand_total = decay * grand_total + jnp.sum(expo, axis=-1)
    summed_output = decay[..., None] * summed_output + jnp.einsum(
        "tgrk,kgd->tgrd", expo.astype(jnp.bfloat16), value_rows, preferred_element_type=jnp.float32
    )
    return (fresh, grand_total, summed_output)


def empty_carry(token_count, request_groups):
    return (
        jnp.full((token_count, KEY_VALUE_HEADS, request_groups), NEGATIVE_MASK, jnp.float32),
        jnp.zeros((token_count, KEY_VALUE_HEADS, request_groups), jnp.float32),
        jnp.zeros((token_count, KEY_VALUE_HEADS, request_groups, HEAD_SIZE), jnp.float32),
    )


def on_device(
    hidden,
    queries,
    suffix_kv,
    lengths,
    page_table,
    page_pool,
    w_out,
    w_router,
    routes,
    w_gate,
    w_up,
    w_down,
):
    token_index = hidden.shape[0]
    row_width = KEY_VALUE_HEADS * HEAD_SIZE
    request_groups = QUERY_HEADS // KEY_VALUE_HEADS
    request_count = lax.axis_size("req")
    pool_per_shard = page_pool.shape[0]
    pool_all = pool_per_shard * request_count
    query_matrix = queries.reshape(token_index, KEY_VALUE_HEADS, request_groups, HEAD_SIZE)
    positions = lax.axis_index("exp") * token_index + jnp.arange(token_index, dtype=jnp.int32)
    lens = lengths[0]
    ends = jnp.cumsum(lens)
    starts = ends - lens
    req_of = jnp.sum((positions[:, None] >= ends[None, :]).astype(jnp.int32), axis=1)
    pick = req_of[:, None] == jnp.arange(lens.shape[0], dtype=jnp.int32)[None, :]
    first = jnp.sum(jnp.where(pick, starts[None, :], 0), axis=1)
    counts = jnp.sum(
        (page_table[0][:, :, None] == jnp.arange(pool_all, dtype=jnp.int32)[None, None, :]).astype(
            jnp.float32
        ),
        axis=1,
    )
    query_counts = jnp.dot(pick.astype(jnp.float32), counts, precision=lax.Precision.HIGHEST)
    query_total_set, every_count = (
        lax.all_gather(queries, "req", axis=0, tiled=True),
        lax.all_gather(query_counts.astype(jnp.bfloat16), "req", axis=0, tiled=True),
    )
    query_total_count = query_total_set.shape[0]
    local = lax.dynamic_slice_in_dim(
        every_count, lax.axis_index("req") * pool_per_shard, pool_per_shard, 1
    ).astype(jnp.float32)
    weights = jnp.repeat(local, PAGE_TOKENS, axis=1)
    flattened = page_pool.reshape(pool_per_shard * PAGE_TOKENS, 2 * row_width)
    key_rows = flattened[:, :row_width].reshape(
        pool_per_shard * PAGE_TOKENS, KEY_VALUE_HEADS, HEAD_SIZE
    )
    value_rows = flattened[:, row_width:].reshape(
        pool_per_shard * PAGE_TOKENS, KEY_VALUE_HEADS, HEAD_SIZE
    )
    running_maximum, grand_total, summed_output = fold_scores(
        empty_carry(query_total_count, request_groups),
        query_total_set.reshape(query_total_count, KEY_VALUE_HEADS, request_groups, HEAD_SIZE),
        key_rows,
        value_rows,
        weights,
    )
    peaks, totals, sums = (
        lax.all_to_all(
            running_maximum.reshape(request_count, token_index, KEY_VALUE_HEADS, request_groups),
            "req",
            split_axis=0,
            concat_axis=0,
            tiled=True,
        ),
        lax.all_to_all(
            grand_total.reshape(request_count, token_index, KEY_VALUE_HEADS, request_groups),
            "req",
            split_axis=0,
            concat_axis=0,
            tiled=True,
        ),
        lax.all_to_all(
            summed_output.reshape(
                request_count, token_index, KEY_VALUE_HEADS, request_groups, HEAD_SIZE
            ),
            "req",
            split_axis=0,
            concat_axis=0,
            tiled=True,
        ),
    )
    highest = jnp.max(peaks, axis=0)
    factor = jnp.exp(peaks - highest[None])
    carry = (highest, jnp.sum(factor * totals, axis=0), jnp.sum(factor[..., None] * sums, axis=0))
    segment = lax.all_gather(suffix_kv, "exp", axis=0, tiled=True)
    token_count = segment.shape[0]
    keypos = jnp.arange(token_count, dtype=jnp.int32)
    weights = (
        (keypos[None, :] <= positions[:, None]) & (keypos[None, :] >= first[:, None])
    ).astype(jnp.float32)
    key_rows = segment[:, :row_width].reshape(token_count, KEY_VALUE_HEADS, HEAD_SIZE)
    value_rows = segment[:, row_width:].reshape(token_count, KEY_VALUE_HEADS, HEAD_SIZE)
    running_maximum, grand_total, summed_output = fold_scores(
        carry, query_matrix, key_rows, value_rows, weights
    )
    attended = (
        (summed_output / grand_total[..., None])
        .reshape(token_index, QUERY_HEADS * HEAD_SIZE)
        .astype(jnp.bfloat16)
    )
    projected = jnp.dot(attended, w_out, preferred_element_type=jnp.float32)
    resid = lax.optimization_barrier((hidden.astype(jnp.float32) + projected).astype(jnp.bfloat16))
    resid_f = resid.astype(jnp.float32)
    normed = (resid_f * lax.rsqrt(jnp.mean(resid_f * resid_f, axis=1, keepdims=True) + EPS)).astype(
        jnp.bfloat16
    )
    n_experts = w_router.shape[1]
    logits = jnp.dot(normed, w_router, preferred_element_type=jnp.float32)
    expert_ids = jnp.arange(n_experts, dtype=jnp.int32)
    chosen = jnp.sum(
        jnp.where(routes[:, :, None] == expert_ids[None, None, :], logits[:, None, :], 0.0), axis=2
    )
    gates = jax.nn.softmax(chosen, axis=1)
    capacity = max(2, (5 * token_index * TOP + 4 * n_experts - 1) // (4 * n_experts))
    flat_routes = routes.reshape(-1)
    onehot = (flat_routes[:, None] == expert_ids[None, :]).astype(jnp.int32)
    rank = jnp.sum(jnp.cumsum(onehot, axis=0) * onehot, axis=1) - 1
    slot = flat_routes * capacity + rank
    send = (
        jnp.zeros((n_experts * capacity, D), jnp.bfloat16)
        .at[slot]
        .set(jnp.repeat(normed, TOP, axis=0))
    )
    outgoing = jnp.broadcast_to(
        send.reshape(n_experts, 1, capacity, D), (n_experts, 2, capacity, D)
    ).reshape(2 * n_experts, capacity, D)
    rows = lax.all_to_all(outgoing, ("req", "exp"), split_axis=0, concat_axis=0, tiled=True)
    array_shape = rows.shape
    flat_rows = rows.reshape(-1, D)
    gate_part = jnp.dot(flat_rows, w_gate[0], preferred_element_type=jnp.float32)
    up_part = jnp.dot(flat_rows, w_up[0], preferred_element_type=jnp.float32)
    inner = (jax.nn.silu(gate_part) * up_part).astype(jnp.bfloat16)
    returned = lax.all_to_all(
        jnp.dot(inner, w_down[0], preferred_element_type=jnp.float32)
        .astype(jnp.bfloat16)
        .reshape(array_shape),
        ("req", "exp"),
        split_axis=0,
        concat_axis=0,
        tiled=True,
    )
    halves = jnp.sum(
        returned.reshape(n_experts, 2, capacity, D).astype(jnp.float32), axis=1
    ).reshape(n_experts * capacity, D)
    picked = halves[slot].reshape(token_index, TOP, D)
    moe = jnp.sum(picked * gates[:, :, None], axis=1)
    return (resid_f + moe).astype(jnp.bfloat16)


def solution(mesh):
    placed = (
        P(("req", "exp"), None),
        P(("req", "exp"), None),
        P(("req", "exp"), None),
        P("req", None),
        P("req", None, None),
        P("req", None, None),
        P(),
        P(),
        P(("req", "exp"), None),
        P(("req", "exp"), None, None),
        P(("req", "exp"), None, None),
        P(("req", "exp"), None, None),
    )
    return jax.shard_map(
        on_device, mesh=mesh, in_specs=placed, out_specs=P(("req", "exp"), None), check_vma=False
    )
```

profile of v0, /device:TPU:34, one launch (start us, length us, event | category | flops | bytes accessed | tf_op | source)
XLA Modules:
  0.0 631.7 jit_solution(13155531788352508001)
XLA Ops:
  11.2 12.1 %all_gather.9 = bf16[1024,56]{0,1:T(8,128)(2,1)S(1)} all-gather(bf16[128,56]{0,1:T(8,128)(2,1)S(1)} %convolution_convert_fusion.1), channel_id=1, replica_groups=mesh['req'=8,'exp'=16] {'req'}, dimensions={0}, use_global_device_ids=true | all-gather | bytes 129024 | tf_op jit(solution)/shard_map/all_gather | solution.py:78
  25.1 16.3 %all-gather.3.cloned.1.call-done = bf16[1024,1280]{0,1:T(8,128)(2,1)} async-done(((bf16[128,1280]{0,1:T(8,128)(2,1)}), bf16[1024,1280]{0,1:T(8,128)(2,1)}) %all-gather.3.cloned.1.call-update) | async-done | bytes 2621456 | tf_op jit(solution)/shard_map/all_gather | solution.py:77
  41.4 16.3 %fusion = (f32[1024,2,5]{0,2,1:T(8,128)S(1)}, f32[2,896,1024,5]{2,1,3,0:T(8,128)}) fusion(pred[1024,896]{0,1:T(8,128)(4,1)S(1)} %bitcast_compare_fusion, bf16[896,2,128,1]{0,2,3,1:T(8,128)(2,1)S(1)} %bitcast.144, bf16[1024,2,5,128]{0,3,2,1:T(8,128)(2,1)} %bitcast.140), kind=kOutput, calls=%fused_computation.4 | convolution fusion | flops 2376325120 | bytes 40738816 | tf_op jit(solution)/shard_map/tgrd,kgd->tgrk/dot_general | solution.py:18
  60.0 15.7 %fusion.4 = f32[1024,2,5]{0,2,1:T(8,128)S(1)} fusion(f32[2,896,1024,5]{2,1,3,0:T(8,128)} %get-tuple-element.18, f32[1024,896]{0,1:T(8,128)S(1)} %bitcast.138, f32[1024,2,5]{0,2,1:T(8,128)S(1)} %get-tuple-element.14, pred[1024,896]{0,1:T(8,128)(4,1)S(1)} %bitcast_compare_fusion), kind=kLoop, calls=%fused_computation.8 | loop fusion | flops 45864960 | bytes 41369600 | tf_op jit(solution)/shard_map/reduce_sum | solution.py:26
  89.2 17.4 %bitcast_add_fusion = f32[1024,2,5,128]{3,0,2,1:T(8,128)S(1)} fusion(f32[1024,2,5]{0,2,1:T(8,128)S(1)} %get-tuple-element.13, bf16[896,2,128,1]{0,2,3,1:T(8,128)(2,1)S(1)} %bitcast.148, f32[2,896,1024,5]{2,1,3,0:T(8,128)} %get-tuple-element.18, f32[1024,896]{0,1:T(8,128)} %bitcast.139, f32[1024,2,5]{0,2,1:T(8,128)S(1)} %get-tuple-element.14, ...), kind=kOutput, calls=%fused_computation.24 | convolution fusion | flops 2395996160 | bytes 47071232 | tf_op jit(solution)/shard_map/tgrk,kgd->tgrd/dot_general | solution.py:27
  117.9 12.6 %all-gather.5.cloned.1.call-done = bf16[2048,512]{0,1:T(8,128)(2,1)} async-done(((bf16[128,512]{0,1:T(8,128)(2,1)}), bf16[2048,512]{0,1:T(8,128)(2,1)}) %all-gather.5.cloned.1.call-update) | async-done | bytes 2097168 | tf_op jit(solution)/shard_map/all_gather | solution.py:127
  145.7 29.8 %all-to-all-done.1 = f32[8,128,2,5,128]{4,1,3,2,0:T(8,128)} async-done(((f32[8,128,2,5,128]{4,1,3,2,0:T(8,128)}), f32[8,128,2,5,128]{4,1,3,2,0:T(8,128)}, u32[]{:S(2)}, u32[]{:S(2)}) %all-to-all-start.1) | async-done | bytes 5242912 | tf_op jit(solution)/shard_map/all_to_all | solution.py:114
  181.9 7.9 %fusion.43 = bf16[128,2,5,128]{0,3,2,1:T(8,128)(2,1)S(1)} fusion(bf16[2048,2,128,1]{0,2,3,1:T(8,128)(2,1)} %bitcast.146, f32[2,2048,128,5]{2,1,3,0:T(8,128)} %get-tuple-element.20, f32[128,2048]{0,1:T(8,128)} %copy-done.3, f32[128,2,5]{0,2,1:T(8,128)S(1)} %copy.180, pred[128,2048]{0,1:T(8,128)(4,1)S(1)} %get-tuple-element.15, ...), kind=kOutput, calls=%fused_computation.52 | convolution fusion | flops 684851200 | bytes 13843456 | tf_op jit(solution)/shard_map/tgrk,kgd->tgrd/dot_general | solution.py:27
  194.2 7.5 %reshape.302 = bf16[768,2560]{1,0:T(8,128)(2,1)} reshape(bf16[128,6,2560]{2,1,0:T(8,128)(2,1)} %broadcast_in_dim.133) | data formatting | bytes 7864320 | tf_op jit(solution)/shard_map/reshape | solution.py:164
  201.7 12.2 %scatter_custom_fusion = bf16[960,2560]{1,0:T(8,128)(2,1)} fusion(s32[768]{0:T(1024)S(1)} %fusion.56, bf16[768,2560]{1,0:T(8,128)(2,1)} %reshape.302, bf16[]{:T(256)} %constant.29.clone.1), kind=kCustom, calls=%fused_computation.35 | custom fusion | bytes 4915712 | tf_op jit(solution)/shard_map/scatter | solution.py:164
  213.9 7.6 %broadcast_in_dim.134 = bf16[64,15,2560]{2,1,0:T(8,128)(2,1)} reshape(bf16[960,2560]{1,0:T(8,128)(2,1)} %scatter_custom_fusion) | data formatting | bytes 9830400 | tf_op jit(solution)/shard_map/broadcast_in_dim | solution.py:166
  221.4 7.8 %broadcast_in_dim.135 = bf16[64,2,15,2560]{3,2,1,0:T(8,128)(2,1)} broadcast(bf16[64,15,2560]{2,1,0:T(8,128)(2,1)} %broadcast_in_dim.134), dimensions={0,2,3} | broadcast | bytes 14745600 | tf_op jit(solution)/shard_map/broadcast_in_dim | solution.py:166
  229.2 127.0 %all_to_all.25 = bf16[128,15,2560]{2,1,0:T(8,128)(2,1)} all-to-all(bf16[128,15,2560]{2,1,0:T(8,128)(2,1)} %bitcast.135), channel_id=1, replica_groups=mesh['req'=8,'exp'=16] {'req','exp'}, dimensions={0} | all-to-all | bytes 19660800 | tf_op jit(solution)/shard_map/all_to_all | solution.py:169
  356.2 13.9 %reshape.285 = bf16[1920,2560]{1,0:T(8,128)(2,1)} reshape(bf16[128,15,2560]{2,1,0:T(8,128)(2,1)} %all_to_all.25) | data formatting | bytes 19660800 | tf_op jit(solution)/shard_map/reshape | solution.py:171
  370.1 13.1 %fusion.21 = f32[1920,768]{1,0:T(8,128)} fusion(bf16[1920,2560]{1,0:T(8,128)(2,1)} %reshape.285, bf16[1,2560,768]{2,1,0:T(8,128)(2,1)} %param.21), kind=kOutput, calls=%fused_computation.30 | convolution fusion | flops 7549747200 | bytes 19660800 | tf_op jit(solution)/shard_map/dot_general | solution.py:172
  383.2 27.3 %convolution_convert_fusion = bf16[1920,2560]{1,0:T(8,128)(2,1)} fusion(f32[1920,768]{1,0:T(8,128)} %fusion.21, bf16[1920,2560]{1,0:T(8,128)(2,1)} %reshape.285, bf16[1,768,2560]{2,1,0:T(8,128)(2,1)} %param.23, bf16[1,2560,768]{2,1,0:T(8,128)(2,1)} %param.22), kind=kOutput, calls=%fused_computation.13 | convolution fusion | flops 15113256960 | bytes 33423360 | tf_op jit(solution)/shard_map/dot_general | solution.py:176
  410.5 13.8 %reshape.286 = bf16[128,15,2560]{2,1,0:T(8,128)(2,1)} reshape(bf16[1920,2560]{1,0:T(8,128)(2,1)} %convolution_convert_fusion) | data formatting | bytes 19660800 | tf_op jit(solution)/shard_map/reshape | solution.py:178
  424.3 7.0 %all-to-all-start.4 = ((bf16[128,15,2560]{2,1,0:T(8,128)(2,1)}), bf16[128,15,2560]{2,1,0:T(8,128)(2,1)}, u32[]{:S(2)}, u32[]{:S(2)}) async-start(bf16[128,15,2560]{2,1,0:T(8,128)(2,1)} %reshape.286), calls=%async_computation.4 | async-start | bytes 20971520 | tf_op jit(solution)/shard_map/all_to_all | solution.py:175
  431.9 140.3 %all-to-all-done.4 = bf16[128,15,2560]{2,1,0:T(8,128)(2,1)} async-done(((bf16[128,15,2560]{2,1,0:T(8,128)(2,1)}), bf16[128,15,2560]{2,1,0:T(8,128)(2,1)}, u32[]{:S(2)}, u32[]{:S(2)}) %all-to-all-start.4) | async-done | bytes 9830432 | tf_op jit(solution)/shard_map/all_to_all | solution.py:175
  572.1 11.3 %convert_reduce_fusion = f32[64,15,2560]{2,1,0:T(8,128)} fusion(bf16[128,15,2560]{2,1,0:T(8,128)(2,1)} %all-to-all-done.4), kind=kLoop, calls=%fused_computation.10 | loop fusion | flops 7372800 | bytes 19660800 | tf_op jit(solution)/shard_map/reduce_sum | solution.py:184
  583.5 10.2 %reshape.287 = f32[960,2560]{1,0:T(8,128)} reshape(f32[64,15,2560]{2,1,0:T(8,128)} %convert_reduce_fusion) | data formatting | bytes 19660800 | tf_op jit(solution)/shard_map/reshape | solution.py:186
  593.7 12.2 %gather_fusion = f32[768,2560]{1,0:T(8,128)} fusion(f32[960,2560]{1,0:T(8,128)} %reshape.287, s32[1024]{0:T(1024)S(1)} %pad_clamp_fusion), kind=kCustom, calls=%fused_computation | custom fusion | bytes 15731712 | tf_op jit(solution)/shard_map/gather | solution.py:187
  605.9 9.2 %reshape.288 = f32[128,6,2560]{2,1,0:T(8,128)} reshape(f32[768,2560]{1,0:T(8,128)} %gather_fusion) | data formatting | bytes 15728640 | tf_op jit(solution)/shard_map/reshape | solution.py:187
  615.2 7.9 %multiply_reduce_fusion = f32[128,2560]{1,0:T(8,128)S(1)} fusion(f32[128,6,2560]{2,1,0:T(8,128)} %reshape.288, f32[128,6]{1,0:T(8,128)S(1)} %copy.192), kind=kLoop, calls=%fused_computation.20 | loop fusion | flops 3604480 | bytes 9178112 | tf_op jit(solution)/shard_map/reduce_sum | solution.py:188
  (93 shorter events, 59.9 us)
Async XLA Ops:
  7.4 424.0 %copy-start = (bf16[2560,64]{0,1:T(8,128)(2,1)S(1)}, bf16[2560,64]{0,1:T(8,128)(2,1)}, u32[]{:S(2)}) copy-start(bf16[2560,64]{0,1:T(8,128)(2,1)} %param.19) | copy-start | bytes 983044
  7.4 34.0 %all-gather.3.cloned.1.call-start = ((), (), s32[]{:S(2)}) async-start(), calls=%async_computation.5 | async-start | bytes 2949120 | tf_op jit(solution)/shard_map/all_gather | solution.py:77
  58.2 1.8 copy-start.1
  60.0 20.4 %copy-start.5 = (bf16[128,512]{1,0:T(8,128)(2,1)S(1)}, bf16[128,512]{1,0:T(8,128)(2,1)}, u32[]{:S(2)}) copy-start(bf16[128,512]{1,0:T(8,128)(2,1)} %param.14) | copy-start | bytes 393220
  76.3 9.5 %all-to-all-start.2 = ((f32[8,128,2,5]{1,2,3,0:T(2,128)}), f32[8,128,2,5]{1,2,3,0:T(2,128)S(1)}, u32[]{:S(2)}, u32[]{:S(2)}) async-start(f32[8,128,2,5]{1,2,3,0:T(2,128)} %copy.183), calls=%async_computation.2 | async-start | bytes 81920 | tf_op jit(solution)/shard_map/all_to_all | solution.py:107
  80.3 50.2 %all-gather.5.cloned.1.call-start = ((), (), s32[]{:S(2)}) async-start(), calls=%async_computation.6 | async-start | bytes 2228224 | tf_op jit(solution)/shard_map/all_gather | solution.py:127
  85.8 23.5 %all-to-all-start = ((f32[8,128,2,5]{1,2,3,0:T(2,128)}), f32[8,128,2,5]{1,2,3,0:T(2,128)S(1)}, u32[]{:S(2)}, u32[]{:S(2)}) async-start(f32[8,128,2,5]{1,2,3,0:T(2,128)} %copy.163), calls=%async_computation | async-start | bytes 81920 | tf_op jit(solution)/shard_map/all_to_all | solution.py:100
  109.3 5.1 copy-start.6
  109.4 8.1 %copy-start.7 = (s32[1,4]{1,0:T(1,128)S(1)}, s32[1,4]{1,0:T(1,128)}, u32[]{:S(2)}) copy-start(s32[1,4]{1,0:T(1,128)} %param.15) | copy-start | bytes 52
  109.4 23.9 %copy-start.2 = (bf16[128,1280]{0,1:T(8,128)(2,1)S(1)}, bf16[128,1280]{0,1:T(8,128)(2,1)}, u32[]{:S(2)}) copy-start(bf16[128,1280]{0,1:T(8,128)(2,1)} %copy.159) | copy-start | bytes 983044
  109.4 66.1 %all-to-all-start.1 = ((f32[8,128,2,5,128]{4,1,3,2,0:T(8,128)}), f32[8,128,2,5,128]{4,1,3,2,0:T(8,128)}, u32[]{:S(2)}, u32[]{:S(2)}) async-start(f32[8,128,2,5,128]{4,1,3,2,0:T(8,128)} %copy.177), calls=%async_computation.1 | async-start | bytes 10485760 | tf_op jit(solution)/shard_map/all_to_all | solution.py:114
  117.9 21.3 %copy-start.3 = (f32[128,2048]{0,1:T(8,128)}, f32[128,2048]{0,1:T(8,128)S(1)}, u32[]{:S(2)}) copy-start(f32[128,2048]{0,1:T(8,128)S(1)} %get-tuple-element.16) | copy-start | bytes 3145732
  175.4 14.4 %slice-start = ((s8[6553600]{0:T(1024)(128)(4,1)}), s8[2359296]{0:T(1024)(128)(4,1)S(1)}, s32[]{:S(2)}) async-start(s8[6553600]{0:T(1024)(128)(4,1)} %bitcast.136), calls=%async_computation.7 | async-start | bytes 4718592
  181.9 7.9 %slice-start.1 = ((s8[6553600]{0:T(1024)(128)(4,1)}), s8[4194304]{0:T(1024)(128)(4,1)S(1)}, s32[]{:S(2)}) async-start(s8[6553600]{0:T(1024)(128)(4,1)} %bitcast.136), calls=%async_computation.8 | async-start | bytes 8388608
  181.9 7.9 %copy-start.4 = (bf16[128,2560]{1,0:T(8,128)(2,1)S(1)}, bf16[128,2560]{1,0:T(8,128)(2,1)}, u32[]{:S(2)}) copy-start(bf16[128,2560]{1,0:T(8,128)(2,1)} %param.12) | copy-start | bytes 1966084
  424.3 147.8 %all-to-all-start.4 = ((bf16[128,15,2560]{2,1,0:T(8,128)(2,1)}), bf16[128,15,2560]{2,1,0:T(8,128)(2,1)}, u32[]{:S(2)}, u32[]{:S(2)}) async-start(bf16[128,15,2560]{2,1,0:T(8,128)(2,1)} %reshape.286), calls=%async_computation.4 | async-start | bytes 20971520 | tf_op jit(solution)/shard_map/all_to_all | solution.py:175
Sparse Core Ops, SparseCore 0:
  9.9 31.4 all-gather.2
Sparse Core Ops, SparseCore 1:
  82.9 47.5 all-gather.4
where the time goes:
time: 642 us; the launch traced here: 632 us
  waiting for transfers between devices  203 us (32%)
  blocking collectives  139 us (22%)
  local copies, waits for them, and re-layouts  114 us (18%)
  matrix products  89.5 us (14%)
  other arithmetic  51.6 us (8%)
  starting transfers between devices  19.5 us (3%)
  between operations  15.4 us (2%)
    all_to_all x1, waiting for transfers between devices, on_device(): lax.all_to_all(jnp.dot(inner, w_down[0], preferred_element_type=jnp.float...  140 us
    all_to_all x1, blocking collectives, on_device(): lax.all_to_all(outgoing, ('req', 'exp'), split_axis=0, concat_axis=0, til...  127 us
    all_to_all x1, waiting for transfers between devices, on_device(): lax.all_to_all(summed_output.reshape(request_count, token_index, KEY_VALU...  29.8 us
    dot_general x1, matrix products, on_device(): jnp.dot(inner, w_down[0], preferred_element_type=jnp.float32)  27.3 us
    dot_general x2, matrix products, fold_scores(): jnp.einsum('tgrk,kgd->tgrd', expo.astype(jnp.bfloat16), value_rows, prefe...  25.3 us
    dot_general x2, matrix products, fold_scores(): jnp.einsum('tgrd,kgd->tgrk', query_matrix, key_rows, preferred_element_ty...  22.1 us
    reduce_sum x2, other arithmetic, fold_scores(): grand_total = decay * grand_total + jnp.sum(expo, axis=-1)  22.1 us
    all_gather x1, waiting for transfers between devices, on_device(): lax.all_gather(queries, 'req', axis=0, tiled=True)  16.3 us
  transfers between devices with their start and end apart: 6, of which 5 were waited for; matrix products, arithmetic and copies ran while one was open for 7% of the time, Pallas kernels for 0%

commit v1 on v0

--- a/solution.py
+++ b/solution.py
@@ -74,7 +74,9 @@
     )
     query_counts = jnp.dot(pick.astype(jnp.float32), counts, precision=lax.Precision.HIGHEST)
     query_total_set, every_count = (
-        lax.all_gather(queries, "req", axis=0, tiled=True),
+        jnp.concatenate(
+            lax.all_to_all(jnp.stack([queries] * lax.axis_size("req")), "req", 0, 0), axis=0
+        ),
         lax.all_gather(query_counts.astype(jnp.bfloat16), "req", axis=0, tiled=True),
     )
     query_total_count = query_total_set.shape[0]

time: 642 us -> 667 us (1.039)
  blocking collectives: 139 us -> 165 us
  local copies, waits for them, and re-layouts: 114 us -> 132 us
  waiting for transfers between devices: 203 us -> 190 us
    all_gather x1, blocking collectives: 12.1 us -> 37.5 us  [on_device(): lax.all_gather(query_counts.astype(jnp.bfloat16), 'req', axis=0, tiled=True)]
    all_gather x1 -> x0, waiting for transfers between devices: 16.3 us -> none  [on_device(): lax.all_gather(queries, 'req', axis=0, tiled=True)]
    all_to_all x0 -> x1, local copies, waits for them, and re-layouts: none -> 9.19 us  [on_device(): lax.all_to_all(jnp.stack([queries] * lax.axis_size('req')), 'req', 0, 0)]
    another operation x0 -> x2, local copies, waits for them, and re-layouts: none -> 7.05 us  [the longest x1 5.18 us: on_device(): query_total_set.reshape(query_total_count, KEY_VALUE_HEADS, request_group...]
  transfers between devices with their start and end apart: 6 -> 6, of which waited for: 5 -> 4; matrix products, arithmetic and copies ran while one was open for 7% -> 5% of each run, Pallas kernels for 0% -> 0%
where the time goes in v1:
time: 667 us; the launch traced here: 657 us
  waiting for transfers between devices  190 us (28%)
  blocking collectives  165 us (25%)
  local copies, waits for them, and re-layouts  132 us (20%)
  matrix products  85.6 us (13%)
  other arithmetic  46.3 us (7%)
  starting transfers between devices  23.1 us (3%)
  between operations  14 us (2%)
    all_to_all x1, waiting for transfers between devices, on_device(): lax.all_to_all(jnp.dot(inner, w_down[0], preferred_element_type=jnp.float...  140 us
    all_to_all x1, blocking collectives, on_device(): lax.all_to_all(outgoing, ('req', 'exp'), split_axis=0, concat_axis=0, til...  128 us
    all_gather x1, blocking collectives, on_device(): lax.all_gather(query_counts.astype(jnp.bfloat16), 'req', axis=0, tiled=True)  37.5 us
    all_to_all x1, waiting for transfers between devices, on_device(): lax.all_to_all(summed_output.reshape(request_count, token_index, KEY_VALU...  32.4 us
    dot_general x1, matrix products, on_device(): jnp.dot(inner, w_down[0], preferred_element_type=jnp.float32)  27.3 us
    dot_general x2, matrix products, fold_scores(): jnp.einsum('tgrk,kgd->tgrd', expo.astype(jnp.bfloat16), value_rows, prefe...  25.3 us
    dot_general x2, matrix products, fold_scores(): jnp.einsum('tgrd,kgd->tgrk', query_matrix, key_rows, preferred_element_ty...  18.2 us
    reduce_sum x2, other arithmetic, fold_scores(): grand_total = decay * grand_total + jnp.sum(expo, axis=-1)  18.1 us
  transfers between devices with their start and end apart: 6, of which 4 were waited for; matrix products, arithmetic and copies ran while one was open for 5% of the time, Pallas kernels for 0%

profile of v1, /device:TPU:34, one launch (start us, length us, event | category | flops | bytes accessed | tf_op | source)
XLA Modules:
  0.0 656.7 jit_solution(15504776445954894416)
XLA Ops:
  14.8 37.5 %all_gather.6 = bf16[1024,56]{0,1:T(8,128)(2,1)S(1)} all-gather(bf16[128,56]{0,1:T(8,128)(2,1)S(1)} %convolution_convert_fusion.1), channel_id=1, replica_groups=mesh['req'=8,'exp'=16] {'req'}, dimensions={0}, use_global_device_ids=true | all-gather | bytes 129024 | tf_op jit(solution)/shard_map/all_gather | solution.py:80
  52.8 9.2 %copy.163 = bf16[8,128,1280]{1,0,2:T(8,128)(2,1)} copy(bf16[8,128,1280]{1,2,0:T(8,128)(2,1)} %all-to-all-done) | data formatting | bytes 5242880 | tf_op jit(solution)/shard_map/all_to_all | solution.py:78
  67.2 16.3 %fusion = (f32[1024,2,5]{0,2,1:T(8,128)S(1)}, f32[2,896,1024,5]{2,1,3,0:T(8,128)}) fusion(pred[1024,896]{0,1:T(8,128)(4,1)S(1)} %bitcast_compare_fusion, bf16[896,2,128,1]{0,2,3,1:T(8,128)(2,1)S(1)} %bitcast.144, bf16[1024,2,5,128]{0,3,2,1:T(8,128)(2,1)} %reshape_reshape.3), kind=kOutput, calls=%fused_computation.4 | convolution fusion | flops 2376325120 | bytes 40738816 | tf_op jit(solution)/shard_map/tgrd,kgd->tgrk/dot_general | solution.py:18
  85.8 15.7 %fusion.4 = f32[1024,2,5]{0,2,1:T(8,128)S(1)} fusion(f32[2,896,1024,5]{2,1,3,0:T(8,128)} %get-tuple-element.18, f32[1024,896]{0,1:T(8,128)S(1)} %bitcast.139, f32[1024,2,5]{0,2,1:T(8,128)S(1)} %get-tuple-element.14, pred[1024,896]{0,1:T(8,128)(4,1)S(1)} %bitcast_compare_fusion), kind=kLoop, calls=%fused_computation.8 | loop fusion | flops 45864960 | bytes 41369600 | tf_op jit(solution)/shard_map/reduce_sum | solution.py:26
  114.5 17.5 %bitcast_add_fusion = f32[1024,2,5,128]{3,0,2,1:T(8,128)S(1)} fusion(f32[1024,2,5]{0,2,1:T(8,128)S(1)} %get-tuple-element.13, bf16[896,2,128,1]{0,2,3,1:T(8,128)(2,1)S(1)} %bitcast.148, f32[2,896,1024,5]{2,1,3,0:T(8,128)} %get-tuple-element.18, f32[1024,896]{0,1:T(8,128)} %bitcast.140, f32[1024,2,5]{0,2,1:T(8,128)S(1)} %get-tuple-element.14, ...), kind=kOutput, calls=%fused_computation.24 | convolution fusion | flops 2395996160 | bytes 47071232 | tf_op jit(solution)/shard_map/tgrk,kgd->tgrd/dot_general | solution.py:27
  142.9 14.0 %all-gather.2.cloned.1.call-done = bf16[2048,512]{0,1:T(8,128)(2,1)} async-done(((bf16[128,512]{0,1:T(8,128)(2,1)}), bf16[2048,512]{0,1:T(8,128)(2,1)}) %all-gather.2.cloned.1.call-update) | async-done | bytes 2097168 | tf_op jit(solution)/shard_map/all_gather | solution.py:129
  168.0 32.4 %all-to-all-done.2 = f32[8,128,2,5,128]{4,1,3,2,0:T(8,128)} async-done(((f32[8,128,2,5,128]{4,1,3,2,0:T(8,128)}), f32[8,128,2,5,128]{4,1,3,2,0:T(8,128)}, u32[]{:S(2)}, u32[]{:S(2)}) %all-to-all-start.2) | async-done | bytes 5242912 | tf_op jit(solution)/shard_map/all_to_all | solution.py:116
  206.9 7.9 %fusion.43 = bf16[128,2,5,128]{0,3,2,1:T(8,128)(2,1)S(1)} fusion(bf16[2048,2,128,1]{0,2,3,1:T(8,128)(2,1)} %bitcast.146, f32[2,2048,128,5]{2,1,3,0:T(8,128)} %copy-done.1, f32[128,2048]{0,1:T(8,128)} %copy-done.3, f32[128,2,5]{0,2,1:T(8,128)S(1)} %copy.184, pred[128,2048]{0,1:T(8,128)(4,1)S(1)} %get-tuple-element.15, f32[128,2,5,128]{0,3,2,1:T(8,128)} %copy.183, ...), kind=kOutput, calls=%fused_computation.52 | convolution fusion | flops 684851200 | bytes 13843456 | tf_op jit(solution)/shard_map/tgrk,kgd->tgrd/dot_general | solution.py:27
  219.2 7.5 %reshape.300 = bf16[768,2560]{1,0:T(8,128)(2,1)} reshape(bf16[128,6,2560]{2,1,0:T(8,128)(2,1)} %broadcast_in_dim.133) | data formatting | bytes 7864320 | tf_op jit(solution)/shard_map/reshape | solution.py:166
  226.7 12.2 %scatter_custom_fusion = bf16[960,2560]{1,0:T(8,128)(2,1)} fusion(s32[768]{0:T(1024)S(1)} %fusion.56, bf16[768,2560]{1,0:T(8,128)(2,1)} %reshape.300, bf16[]{:T(256)} %constant.29.clone.1), kind=kCustom, calls=%fused_computation.35 | custom fusion | bytes 4915712 | tf_op jit(solution)/shard_map/scatter | solution.py:166
  238.9 7.6 %broadcast_in_dim.134 = bf16[64,15,2560]{2,1,0:T(8,128)(2,1)} reshape(bf16[960,2560]{1,0:T(8,128)(2,1)} %scatter_custom_fusion) | data formatting | bytes 9830400 | tf_op jit(solution)/shard_map/broadcast_in_dim | solution.py:168
  246.4 7.8 %broadcast_in_dim.135 = bf16[64,2,15,2560]{3,2,1,0:T(8,128)(2,1)} broadcast(bf16[64,15,2560]{2,1,0:T(8,128)(2,1)} %broadcast_in_dim.134), dimensions={0,2,3} | broadcast | bytes 14745600 | tf_op jit(solution)/shard_map/broadcast_in_dim | solution.py:168
  254.2 127.5 %all_to_all.30 = bf16[128,15,2560]{2,1,0:T(8,128)(2,1)} all-to-all(bf16[128,15,2560]{2,1,0:T(8,128)(2,1)} %bitcast.136), channel_id=1, replica_groups=mesh['req'=8,'exp'=16] {'req','exp'}, dimensions={0} | all-to-all | bytes 19660800 | tf_op jit(solution)/shard_map/all_to_all | solution.py:171
  381.8 13.9 %reshape.283 = bf16[1920,2560]{1,0:T(8,128)(2,1)} reshape(bf16[128,15,2560]{2,1,0:T(8,128)(2,1)} %all_to_all.30) | data formatting | bytes 19660800 | tf_op jit(solution)/shard_map/reshape | solution.py:173
  395.7 13.1 %fusion.21 = f32[1920,768]{1,0:T(8,128)} fusion(bf16[1920,2560]{1,0:T(8,128)(2,1)} %reshape.283, bf16[1,2560,768]{2,1,0:T(8,128)(2,1)} %param.21), kind=kOutput, calls=%fused_computation.30 | convolution fusion | flops 7549747200 | bytes 19660800 | tf_op jit(solution)/shard_map/dot_general | solution.py:174
  408.8 27.3 %convolution_convert_fusion = bf16[1920,2560]{1,0:T(8,128)(2,1)} fusion(f32[1920,768]{1,0:T(8,128)} %fusion.21, bf16[1920,2560]{1,0:T(8,128)(2,1)} %reshape.283, bf16[1,768,2560]{2,1,0:T(8,128)(2,1)} %param.23, bf16[1,2560,768]{2,1,0:T(8,128)(2,1)} %param.22), kind=kOutput, calls=%fused_computation.13 | convolution fusion | flops 15113256960 | bytes 33423360 | tf_op jit(solution)/shard_map/dot_general | solution.py:178
  436.1 13.8 %reshape.284 = bf16[128,15,2560]{2,1,0:T(8,128)(2,1)} reshape(bf16[1920,2560]{1,0:T(8,128)(2,1)} %convolution_convert_fusion) | data formatting | bytes 19660800 | tf_op jit(solution)/shard_map/reshape | solution.py:180
  449.9 7.0 %all-to-all-start.5 = ((bf16[128,15,2560]{2,1,0:T(8,128)(2,1)}), bf16[128,15,2560]{2,1,0:T(8,128)(2,1)}, u32[]{:S(2)}, u32[]{:S(2)}) async-start(bf16[128,15,2560]{2,1,0:T(8,128)(2,1)} %reshape.284), calls=%async_computation.5 | async-start | bytes 20971520 | tf_op jit(solution)/shard_map/all_to_all | solution.py:177
  457.5 140.3 %all-to-all-done.5 = bf16[128,15,2560]{2,1,0:T(8,128)(2,1)} async-done(((bf16[128,15,2560]{2,1,0:T(8,128)(2,1)}), bf16[128,15,2560]{2,1,0:T(8,128)(2,1)}, u32[]{:S(2)}, u32[]{:S(2)}) %all-to-all-start.5) | async-done | bytes 9830432 | tf_op jit(solution)/shard_map/all_to_all | solution.py:177
  597.7 11.3 %convert_reduce_fusion = f32[64,15,2560]{2,1,0:T(8,128)} fusion(bf16[128,15,2560]{2,1,0:T(8,128)(2,1)} %all-to-all-done.5), kind=kLoop, calls=%fused_computation.10 | loop fusion | flops 7372800 | bytes 19660800 | tf_op jit(solution)/shard_map/reduce_sum | solution.py:186
  609.1 10.2 %reshape.285 = f32[960,2560]{1,0:T(8,128)} reshape(f32[64,15,2560]{2,1,0:T(8,128)} %convert_reduce_fusion) | data formatting | bytes 19660800 | tf_op jit(solution)/shard_map/reshape | solution.py:188
  619.3 12.2 %gather_fusion = f32[768,2560]{1,0:T(8,128)} fusion(f32[960,2560]{1,0:T(8,128)} %reshape.285, s32[1024]{0:T(1024)S(1)} %pad_clamp_fusion), kind=kCustom, calls=%fused_computation | custom fusion | bytes 15731712 | tf_op jit(solution)/shard_map/gather | solution.py:189
  631.5 9.2 %reshape.286 = f32[128,6,2560]{2,1,0:T(8,128)} reshape(f32[768,2560]{1,0:T(8,128)} %gather_fusion) | data formatting | bytes 15728640 | tf_op jit(solution)/shard_map/reshape | solution.py:189
  640.8 7.9 %multiply_reduce_fusion = f32[128,2560]{1,0:T(8,128)S(1)} fusion(f32[128,6,2560]{2,1,0:T(8,128)} %reshape.286, f32[128,6]{1,0:T(8,128)S(1)} %copy.196), kind=kLoop, calls=%fused_computation.20 | loop fusion | flops 3604480 | bytes 9178112 | tf_op jit(solution)/shard_map/reduce_sum | solution.py:190
  (99 shorter events, 63.4 us)
Async XLA Ops:
  6.5 450.4 %copy-start = (bf16[2560,64]{0,1:T(8,128)(2,1)S(1)}, bf16[2560,64]{0,1:T(8,128)(2,1)}, u32[]{:S(2)}) copy-start(bf16[2560,64]{0,1:T(8,128)(2,1)} %param.19) | copy-start | bytes 983044
  6.5 7.6 %copy-start.9 = (s32[1,4]{1,0:T(1,128)S(1)}, s32[1,4]{1,0:T(1,128)}, u32[]{:S(2)}) copy-start(s32[1,4]{1,0:T(1,128)} %param.15) | copy-start | bytes 52
  6.5 7.9 %copy-start.8 = (s32[1,4,32]{2,1,0:T(4,128)S(1)}, s32[1,4,32]{2,1,0:T(4,128)}, u32[]{:S(2)}) copy-start(s32[1,4,32]{2,1,0:T(4,128)} %param.16) | copy-start | bytes 1540
  6.5 45.9 %copy-start.4 = (bf16[7,128,512]{2,1,0:T(8,128)(2,1)S(1)}, bf16[7,128,512]{2,1,0:T(8,128)(2,1)}, u32[]{:S(2)}) copy-start(bf16[7,128,512]{2,1,0:T(8,128)(2,1)} %param.17) | copy-start | bytes 2752516
  9.7 43.1 %all-to-all-start = ((bf16[8,128,1280]{1,2,0:T(8,128)(2,1)}), bf16[8,128,1280]{1,2,0:T(8,128)(2,1)}, u32[]{:S(2)}, u32[]{:S(2)}) async-start(bf16[8,128,1280]{1,2,0:T(8,128)(2,1)} %stack.2), calls=%async_computation | async-start | bytes 5242880 | tf_op jit(solution)/shard_map/all_to_all | solution.py:78
  84.0 1.8 copy-start.2
  85.8 19.8 %copy-start.6 = (bf16[128,512]{1,0:T(8,128)(2,1)S(1)}, bf16[128,512]{1,0:T(8,128)(2,1)}, u32[]{:S(2)}) copy-start(bf16[128,512]{1,0:T(8,128)(2,1)} %param.14) | copy-start | bytes 393220
  102.2 8.8 %all-to-all-start.3 = ((f32[8,128,2,5]{1,2,3,0:T(2,128)}), f32[8,128,2,5]{1,2,3,0:T(2,128)S(1)}, u32[]{:S(2)}, u32[]{:S(2)}) async-start(f32[8,128,2,5]{1,2,3,0:T(2,128)} %copy.187), calls=%async_computation.3 | async-start | bytes 81920 | tf_op jit(solution)/shard_map/all_to_all | solution.py:109
  105.5 51.4 %all-gather.2.cloned.1.call-start = ((), (), s32[]{:S(2)}) async-start(), calls=%async_computation.6 | async-start | bytes 2228224 | tf_op jit(solution)/shard_map/all_gather | solution.py:129
  110.9 23.7 %all-to-all-start.1 = ((f32[8,128,2,5]{1,2,3,0:T(2,128)}), f32[8,128,2,5]{1,2,3,0:T(2,128)S(1)}, u32[]{:S(2)}, u32[]{:S(2)}) async-start(f32[8,128,2,5]{1,2,3,0:T(2,128)} %copy.167), calls=%async_computation.1 | async-start | bytes 81920 | tf_op jit(solution)/shard_map/all_to_all | solution.py:102
  131.9 7.5 %copy-start.7 = (s32[128,6]{0,1:T(8,128)S(1)}, s32[128,6]{0,1:T(8,128)}, u32[]{:S(2)}) copy-start(s32[128,6]{0,1:T(8,128)} %param.20) | copy-start | bytes 9220
  134.7 65.8 %all-to-all-start.2 = ((f32[8,128,2,5,128]{4,1,3,2,0:T(8,128)}), f32[8,128,2,5,128]{4,1,3,2,0:T(8,128)}, u32[]{:S(2)}, u32[]{:S(2)}) async-start(f32[8,128,2,5,128]{4,1,3,2,0:T(8,128)} %copy.181), calls=%async_computation.2 | async-start | bytes 10485760 | tf_op jit(solution)/shard_map/all_to_all | solution.py:116
  142.8 18.7 %copy-start.3 = (f32[128,2048]{0,1:T(8,128)}, f32[128,2048]{0,1:T(8,128)S(1)}, u32[]{:S(2)}) copy-start(f32[128,2048]{0,1:T(8,128)S(1)} %get-tuple-element.16) | copy-start | bytes 3145732
  161.5 4.0 copy-start.1
  200.4 14.4 %slice-start = ((s8[6553600]{0:T(1024)(128)(4,1)}), s8[2359296]{0:T(1024)(128)(4,1)S(1)}, s32[]{:S(2)}) async-start(s8[6553600]{0:T(1024)(128)(4,1)} %bitcast.137), calls=%async_computation.7 | async-start | bytes 4718592
  206.9 7.9 %slice-start.1 = ((s8[6553600]{0:T(1024)(128)(4,1)}), s8[4194304]{0:T(1024)(128)(4,1)S(1)}, s32[]{:S(2)}) async-start(s8[6553600]{0:T(1024)(128)(4,1)} %bitcast.137), calls=%async_computation.8 | async-start | bytes 8388608
  206.9 7.9 %copy-start.5 = (bf16[128,2560]{1,0:T(8,128)(2,1)S(1)}, bf16[128,2560]{1,0:T(8,128)(2,1)}, u32[]{:S(2)}) copy-start(bf16[128,2560]{1,0:T(8,128)(2,1)} %param.12) | copy-start | bytes 1966084
  449.9 147.8 %all-to-all-start.5 = ((bf16[128,15,2560]{2,1,0:T(8,128)(2,1)}), bf16[128,15,2560]{2,1,0:T(8,128)(2,1)}, u32[]{:S(2)}, u32[]{:S(2)}) async-start(bf16[128,15,2560]{2,1,0:T(8,128)(2,1)} %reshape.284), calls=%async_computation.5 | async-start | bytes 20971520 | tf_op jit(solution)/shard_map/all_to_all | solution.py:177
Sparse Core Ops, SparseCore 0:
  108.5 48.3 all-gather.1
